TPU v7x, 32 devices: a whole 2x2x4 slice. The times are simulated.
32 devices in a mesh: sub: 2 (over x), section: 4 (over y, core), iface: 4 (over z).
Axes of the slice: x: 2, y: 2, z: 4, core: 2. Of those that a mesh axis runs over, the one named last changes fastest.
Arguments:
- previous: float32 [4, 512, 128], P('section', ('sub', 'iface')), may hold values from -6 to 6
- right_side: float32 [4, 512, 128], P('section', ('sub', 'iface')), may hold values from -96 to 96
- precond: bfloat16 [4, 8, 64, 64], P('section', ('sub', 'iface')), may hold values from -1 to 1
- couple: bfloat16 [4, 8, 64, 64], P('section', ('sub', 'iface')), may hold values from -1.5 to 1.5
- block_ids: int32 [4, 8, 8], P('section', ('sub', 'iface')), may hold values from 0 to 7, as said below
- iface_matrix: bfloat16 [4, 8, 512, 512], P('section', ('sub', 'iface')), may hold values from -1 to 2.5
- interior_coupling: bfloat16 [4, 8, 2560, 512], P('section', ('sub', 'iface')), may hold values from -0.08300781 to 0.08300781
- inv_interior: bfloat16 [4, 8, 2560, 2560], P('section', ('sub', 'iface')), may hold values from -1 to 2
Outputs:
- temperatures: float32 [4, 512, 128], P('section', ('sub', 'iface'))
Inputs may be any that keep to these rules, and one draw needn't show every extreme that they name: `block_ids`: each subdomain lists 8 different blocks, and each block of a section is listed by exactly 8 subdomains.
All inputs are finite; a program needn't handle non-finite values.
Results may differ from a plain program's by a relative error of at most 0.0018.
Values may be sent and summed in bfloat16 or wider, within the bound.
No kernel may reach another device: no remote copies, remote signals or barrier semaphores. Data moves between devices by JAX's collectives and lax.ppermute only.
A program may use at most 128 MiB of HBM per device.

v0:
```python
import jax
import jax.numpy as jnp
from jax import lax
from jax.sharding import PartitionSpec as P

SWEEPS = 4


def from_behind(block, axis, distance):
    devices = range(lax.axis_size(axis))
    route = [(i - distance, i) for i in devices if i - distance in devices]
    return lax.ppermute(block, axis, route)


def body(
    previous, right_side, precond, couple, block_ids, iface_matrix, interior_coupling, inv_interior
):
    highest = lax.Precision.HIGHEST
    section_pos = lax.axis_index("section")
    section_count = lax.axis_size("section")
    owners = lax.axis_size(("sub", "iface"))
    block_list = block_ids[0, 0]
    boundary = iface_matrix[0, 0]
    coupled = interior_coupling[0, 0]
    inverse = inv_interior[0, 0]
    bnd_width = boundary.shape[0]
    block_nodes = previous.shape[1]
    load_count = previous.shape[2]
    pick_count = block_list.shape[0]
    spread = (block_list[:, None] == jnp.arange(owners, dtype=jnp.int32)[None, :]).astype(
        jnp.float32
    )
    precond_f = precond[0].astype(jnp.float32)
    couple_f = couple[0].astype(jnp.float32)
    temps_now = previous
    for sweep_index in range(SWEEPS):
        gathered = lax.all_gather(
            temps_now.astype(jnp.bfloat16), ("sub", "iface"), axis=0, tiled=True
        )
        sub_rows = jnp.take(gathered, block_list, axis=0).reshape(bnd_width, load_count)
        interior_in = jnp.dot(coupled, sub_rows, preferred_element_type=jnp.float32).astype(
            jnp.bfloat16
        )
        interior_out = jnp.dot(inverse, interior_in, preferred_element_type=jnp.float32).astype(
            jnp.bfloat16
        )
        pulled_back = lax.dot_general(
            coupled, interior_out, (((0,), (0,)), ((), ())), preferred_element_type=jnp.float32
        )
        sub_term = jnp.dot(boundary, sub_rows, preferred_element_type=jnp.float32) - pulled_back
        terms = jnp.einsum(
            "kn,kil->nil",
            spread,
            sub_term.reshape(pick_count, block_nodes, load_count),
            precision=highest,
        )
        assembled = lax.psum_scatter(terms, ("sub", "iface"), scatter_dimension=0, tiled=True)
        upper_term = jnp.einsum("bij,bil->bjl", couple_f, temps_now, precision=highest)
        from_above = from_behind(upper_term.astype(jnp.bfloat16), "section", -1).astype(
            upper_term.dtype
        )
        base_resid = right_side - assembled - from_above
        current = temps_now
        for turn_index in range(section_count):
            residual_now = base_resid
            if turn_index > 0:
                below_value = from_behind(current.astype(jnp.bfloat16), "section", 1).astype(
                    current.dtype
                )
                residual_now = base_resid - jnp.einsum(
                    "bij,bjl->bil", couple_f, below_value, precision=highest
                )
            updated = current + jnp.einsum(
                "bij,bjl->bil", precond_f, residual_now, precision=highest
            )
            current = jnp.where(section_pos == turn_index, updated, current)
        temps_now = current
    return temps_now


def solution(mesh):
    in_specs = (
        P("section", ("sub", "iface"), None),
        P("section", ("sub", "iface"), None),
        P("section", ("sub", "iface"), None, None),
        P("section", ("sub", "iface"), None, None),
        P("section", ("sub", "iface"), None),
        P("section", ("sub", "iface"), None, None),
        P("section", ("sub", "iface"), None, None),
        P("section", ("sub", "iface"), None, None),
    )
    out_specs = P("section", ("sub", "iface"), None)
    return jax.shard_map(body, mesh=mesh, in_specs=in_specs, out_specs=out_specs, check_vma=False)
```

profile of v0, /device:TPU:1, one launch (start us, length us, event | category | flops | bytes accessed | tf_op | source)
XLA Modules:
  0.0 516.7 jit_solution(11397847396877441020)
XLA Ops:
  8.8 25.8 %all_gather.12 = bf16[8,64,128]{2,1,0:T(8,128)(2,1)S(1)} all-gather(bf16[1,64,128]{2,1,0:T(8,128)(2,1)S(1)} %convert_element_type.140), channel_id=1, replica_groups=mesh['sub'=2,'section'=4,'iface'=4] {'sub','iface'}, dimensions={0}, use_global_device_ids=true | all-gather | bytes 147456 | tf_op jit(solution)/shard_map/all_gather | solution.py:37
  35.3 10.8 %fusion.8 = bf16[128,2560]{1,0:T(8,128)(2,1)} fusion(bf16[1,1,2560,2560]{3,2,1,0:T(8,128)(2,1)} %param.17, bf16[512,128]{1,0:T(8,128)(2,1)S(1)} %bitcast.529, bf16[1,1,2560,512]{3,2,1,0:T(8,128)(2,1)S(1)} %copy-done), kind=kOutput, calls=%fused_computation.12 | convolution fusion | flops 2013921280 | bytes 16515072 | tf_op jit(solution)/shard_map/dot_general | solution.py:44
  51.3 8.6 %collective-permute-start = (bf16[1,64,128]{2,1,0:T(8,128)(2,1)S(1)}, bf16[1,64,128]{2,1,0:T(8,128)(2,1)S(1)}, u32[]{:S(2)}, u32[]{:S(2)}) collective-permute-start(bf16[1,64,128]{2,1,0:T(8,128)(2,1)S(1)} %fusion.92), channel_id=1, source_target_pairs={{4,0},{8,4},{12,8},{5,1},{9,5},{13,9},{6,2},{10,6},{14,10},{7,3},{... | collective-permute-start | bytes 49160 | tf_op jit(solution)/shard_map/ppermute | solution.py:12
  62.5 55.1 %reduce-scatter.5.cloned.1.call-done = f32[1,64,128]{2,1,0:T(8,128)} async-done(((f32[8,64,128]{2,1,0:T(8,128)}), f32[1,64,128]{2,1,0:T(8,128)}) %reduce-scatter.5.cloned.1.call-update) | async-done | bytes 32784 | tf_op jit(solution)/shard_map/reduce_scatter | solution.py:57
  118.5 5.6 %collective-permute-start.1 = (bf16[1,64,128]{2,1,0:T(8,128)(2,1)S(1)}, bf16[1,64,128]{2,1,0:T(8,128)(2,1)S(1)}, u32[]{:S(2)}, u32[]{:S(2)}) collective-permute-start(bf16[1,64,128]{2,1,0:T(8,128)(2,1)S(1)} %get-tuple-element.6), channel_id=1, source_target_pairs={{0,4},{4,8},{8,12},{1,5},{5,9},{9,13},{2,6},{6,10},{10,14},{3,7},{... | collective-permute-start | bytes 49160 | tf_op jit(solution)/shard_map/ppermute | solution.py:12
  130.6 4.2 collective-permute-start.3
  135.9 24.6 %all_gather.13 = bf16[8,64,128]{2,1,0:T(8,128)(2,1)S(1)} all-gather(bf16[1,64,128]{2,1,0:T(8,128)(2,1)S(1)} %get-tuple-element.12), channel_id=1, replica_groups=mesh['sub'=2,'section'=4,'iface'=4] {'sub','iface'}, dimensions={0}, use_global_device_ids=true | all-gather | bytes 147456 | tf_op jit(solution)/shard_map/all_gather | solution.py:37
  161.2 10.8 %fusion.11 = bf16[128,2560]{1,0:T(8,128)(2,1)} fusion(bf16[1,1,2560,2560]{3,2,1,0:T(8,128)(2,1)} %param.17, bf16[512,128]{1,0:T(8,128)(2,1)S(1)} %bitcast.531, bf16[1,1,2560,512]{3,2,1,0:T(8,128)(2,1)S(1)} %copy-done), kind=kOutput, calls=%fused_computation.13 | convolution fusion | flops 2013921280 | bytes 16515072 | tf_op jit(solution)/shard_map/dot_general | solution.py:44
  177.1 6.3 %collective-permute-start.4 = (bf16[1,64,128]{2,1,0:T(8,128)(2,1)S(1)}, bf16[1,64,128]{2,1,0:T(8,128)(2,1)S(1)}, u32[]{:S(2)}, u32[]{:S(2)}) collective-permute-start(bf16[1,64,128]{2,1,0:T(8,128)(2,1)S(1)} %fusion.93), channel_id=1, source_target_pairs={{4,0},{8,4},{12,8},{5,1},{9,5},{13,9},{6,2},{10,6},{14,10},{7,3},{... | collective-permute-start | bytes 49160 | tf_op jit(solution)/shard_map/ppermute | solution.py:12
  183.3 5.5 %collective-permute-done.4 = bf16[1,64,128]{2,1,0:T(8,128)(2,1)S(1)} collective-permute-done((bf16[1,64,128]{2,1,0:T(8,128)(2,1)S(1)}, bf16[1,64,128]{2,1,0:T(8,128)(2,1)S(1)}, u32[]{:S(2)}, u32[]{:S(2)}) %collective-permute-start.4) | collective-permute-done | bytes 16416 | tf_op jit(solution)/shard_map/ppermute | solution.py:12
  188.9 53.2 %reduce-scatter.7.cloned.1.call-done = f32[1,64,128]{2,1,0:T(8,128)} async-done(((f32[8,64,128]{2,1,0:T(8,128)}), f32[1,64,128]{2,1,0:T(8,128)}) %reduce-scatter.7.cloned.1.call-update) | async-done | bytes 32784 | tf_op jit(solution)/shard_map/reduce_scatter | solution.py:57
  243.0 5.6 %collective-permute-start.5 = (bf16[1,64,128]{2,1,0:T(8,128)(2,1)S(1)}, bf16[1,64,128]{2,1,0:T(8,128)(2,1)S(1)}, u32[]{:S(2)}, u32[]{:S(2)}) collective-permute-start(bf16[1,64,128]{2,1,0:T(8,128)(2,1)S(1)} %get-tuple-element.14), channel_id=1, source_target_pairs={{0,4},{4,8},{8,12},{1,5},{5,9},{9,13},{2,6},{6,10},{10,14},{3,7},{... | collective-permute-start | bytes 49160 | tf_op jit(solution)/shard_map/ppermute | solution.py:12
  260.4 24.9 %all_gather.14 = bf16[8,64,128]{2,1,0:T(8,128)(2,1)S(1)} all-gather(bf16[1,64,128]{2,1,0:T(8,128)(2,1)S(1)} %get-tuple-element.20), channel_id=1, replica_groups=mesh['sub'=2,'section'=4,'iface'=4] {'sub','iface'}, dimensions={0}, use_global_device_ids=true | all-gather | bytes 147456 | tf_op jit(solution)/shard_map/all_gather | solution.py:37
  285.9 10.8 %fusion.14 = bf16[128,2560]{1,0:T(8,128)(2,1)} fusion(bf16[1,1,2560,2560]{3,2,1,0:T(8,128)(2,1)} %param.17, bf16[512,128]{1,0:T(8,128)(2,1)S(1)} %bitcast.533, bf16[1,1,2560,512]{3,2,1,0:T(8,128)(2,1)S(1)} %copy-done), kind=kOutput, calls=%fused_computation.14 | convolution fusion | flops 2013921280 | bytes 16515072 | tf_op jit(solution)/shard_map/dot_general | solution.py:44
  301.8 6.2 %collective-permute-start.8 = (bf16[1,64,128]{2,1,0:T(8,128)(2,1)S(1)}, bf16[1,64,128]{2,1,0:T(8,128)(2,1)S(1)}, u32[]{:S(2)}, u32[]{:S(2)}) collective-permute-start(bf16[1,64,128]{2,1,0:T(8,128)(2,1)S(1)} %fusion.94), channel_id=1, source_target_pairs={{4,0},{8,4},{12,8},{5,1},{9,5},{13,9},{6,2},{10,6},{14,10},{7,3},{... | collective-permute-start | bytes 49160 | tf_op jit(solution)/shard_map/ppermute | solution.py:12
  308.0 5.6 %collective-permute-done.8 = bf16[1,64,128]{2,1,0:T(8,128)(2,1)S(1)} collective-permute-done((bf16[1,64,128]{2,1,0:T(8,128)(2,1)S(1)}, bf16[1,64,128]{2,1,0:T(8,128)(2,1)S(1)}, u32[]{:S(2)}, u32[]{:S(2)}) %collective-permute-start.8) | collective-permute-done | bytes 16416 | tf_op jit(solution)/shard_map/ppermute | solution.py:12
  313.6 53.2 %reduce-scatter.9.cloned.1.call-done = f32[1,64,128]{2,1,0:T(8,128)} async-done(((f32[8,64,128]{2,1,0:T(8,128)}), f32[1,64,128]{2,1,0:T(8,128)}) %reduce-scatter.9.cloned.1.call-update) | async-done | bytes 32784 | tf_op jit(solution)/shard_map/reduce_scatter | solution.py:57
  367.7 5.6 %collective-permute-start.9 = (bf16[1,64,128]{2,1,0:T(8,128)(2,1)S(1)}, bf16[1,64,128]{2,1,0:T(8,128)(2,1)S(1)}, u32[]{:S(2)}, u32[]{:S(2)}) collective-permute-start(bf16[1,64,128]{2,1,0:T(8,128)(2,1)S(1)} %get-tuple-element.22), channel_id=1, source_target_pairs={{0,4},{4,8},{8,12},{1,5},{5,9},{9,13},{2,6},{6,10},{10,14},{3,7},{... | collective-permute-start | bytes 49160 | tf_op jit(solution)/shard_map/ppermute | solution.py:12
  385.1 24.7 %all_gather.15 = bf16[8,64,128]{2,1,0:T(8,128)(2,1)S(1)} all-gather(bf16[1,64,128]{2,1,0:T(8,128)(2,1)S(1)} %get-tuple-element.28), channel_id=1, replica_groups=mesh['sub'=2,'section'=4,'iface'=4] {'sub','iface'}, dimensions={0}, use_global_device_ids=true | all-gather | bytes 147456 | tf_op jit(solution)/shard_map/all_gather | solution.py:37
  410.4 10.8 %fusion.17 = bf16[128,2560]{1,0:T(8,128)(2,1)} fusion(bf16[1,1,2560,2560]{3,2,1,0:T(8,128)(2,1)} %param.17, bf16[512,128]{1,0:T(8,128)(2,1)S(1)} %bitcast.527, bf16[1,1,2560,512]{3,2,1,0:T(8,128)(2,1)S(1)} %copy-done), kind=kOutput, calls=%fused_computation.15 | convolution fusion | flops 2013921280 | bytes 16515072 | tf_op jit(solution)/shard_map/dot_general | solution.py:44
  426.3 6.2 %collective-permute-start.12 = (bf16[1,64,128]{2,1,0:T(8,128)(2,1)S(1)}, bf16[1,64,128]{2,1,0:T(8,128)(2,1)S(1)}, u32[]{:S(2)}, u32[]{:S(2)}) collective-permute-start(bf16[1,64,128]{2,1,0:T(8,128)(2,1)S(1)} %fusion.95), channel_id=1, source_target_pairs={{4,0},{8,4},{12,8},{5,1},{9,5},{13,9},{6,2},{10,6},{14,10},{7,3},{... | collective-permute-start | bytes 49160 | tf_op jit(solution)/shard_map/ppermute | solution.py:12
  432.4 5.6 %collective-permute-done.12 = bf16[1,64,128]{2,1,0:T(8,128)(2,1)S(1)} collective-permute-done((bf16[1,64,128]{2,1,0:T(8,128)(2,1)S(1)}, bf16[1,64,128]{2,1,0:T(8,128)(2,1)S(1)}, u32[]{:S(2)}, u32[]{:S(2)}) %collective-permute-start.12) | collective-permute-done | bytes 16416 | tf_op jit(solution)/shard_map/ppermute | solution.py:12
  438.0 53.3 %reduce-scatter.11.cloned.1.call-done = f32[1,64,128]{2,1,0:T(8,128)} async-done(((f32[8,64,128]{2,1,0:T(8,128)}), f32[1,64,128]{2,1,0:T(8,128)}) %reduce-scatter.11.cloned.1.call-update) | async-done | bytes 32784 | tf_op jit(solution)/shard_map/reduce_scatter | solution.py:57
  492.2 5.5 %collective-permute-start.13 = (bf16[1,64,128]{2,1,0:T(8,128)(2,1)S(1)}, bf16[1,64,128]{2,1,0:T(8,128)(2,1)S(1)}, u32[]{:S(2)}, u32[]{:S(2)}) collective-permute-start(bf16[1,64,128]{2,1,0:T(8,128)(2,1)S(1)} %get-tuple-element.30), channel_id=1, source_target_pairs={{0,4},{4,8},{8,12},{1,5},{5,9},{9,13},{2,6},{6,10},{10,14},{3,7},{... | collective-permute-start | bytes 49160 | tf_op jit(solution)/shard_map/ppermute | solution.py:12
  (110 shorter events, 74.9 us)
Async XLA Ops:
  6.5 28.7 %copy-start = (bf16[1,1,2560,512]{3,2,1,0:T(8,128)(2,1)S(1)}, bf16[1,1,2560,512]{3,2,1,0:T(8,128)(2,1)}, u32[]{:S(2)}) copy-start(bf16[1,1,2560,512]{3,2,1,0:T(8,128)(2,1)} %param.16) | copy-start | bytes 7864324
  6.5 111.1 %reduce-scatter.5.cloned.1.call-start = ((), (), s32[]{:S(2)}) async-start(), calls=%async_computation.4 | async-start | bytes 294912 | tf_op jit(solution)/shard_map/reduce_scatter | solution.py:57
  46.1 5.0 copy-start.5
  46.1 71.5 %copy-start.4 = (f32[1,64,128]{2,1,0:T(8,128)S(1)}, f32[1,64,128]{2,1,0:T(8,128)}, u32[]{:S(2)}) copy-start(f32[1,64,128]{2,1,0:T(8,128)} %param.11) | copy-start | bytes 98308
  46.1 72.3 %copy-start.3 = (bf16[1,1,64,64]{3,2,1,0:T(8,128)(2,1)S(1)}, bf16[1,1,64,64]{3,2,1,0:T(8,128)(2,1)}, u32[]{:S(2)}) copy-start(bf16[1,1,64,64]{3,2,1,0:T(8,128)(2,1)} %param.12) | copy-start | bytes 24580
  51.0 191.1 %reduce-scatter.7.cloned.1.call-start = ((), (), s32[]{:S(2)}) async-start(), calls=%async_computation.5 | async-start | bytes 294912 | tf_op jit(solution)/shard_map/reduce_scatter | solution.py:57
  51.3 11.2 %collective-permute-start = (bf16[1,64,128]{2,1,0:T(8,128)(2,1)S(1)}, bf16[1,64,128]{2,1,0:T(8,128)(2,1)S(1)}, u32[]{:S(2)}, u32[]{:S(2)}) collective-permute-start(bf16[1,64,128]{2,1,0:T(8,128)(2,1)S(1)} %fusion.92), channel_id=1, source_target_pairs={{4,0},{8,4},{12,8},{5,1},{9,5},{13,9},{6,2},{10,6},{14,10},{7,3},{... | collective-permute-start | bytes 49160 | tf_op jit(solution)/shard_map/ppermute | solution.py:12
  118.5 6.4 %collective-permute-start.1 = (bf16[1,64,128]{2,1,0:T(8,128)(2,1)S(1)}, bf16[1,64,128]{2,1,0:T(8,128)(2,1)S(1)}, u32[]{:S(2)}, u32[]{:S(2)}) collective-permute-start(bf16[1,64,128]{2,1,0:T(8,128)(2,1)S(1)} %get-tuple-element.6), channel_id=1, source_target_pairs={{0,4},{4,8},{8,12},{1,5},{5,9},{9,13},{2,6},{6,10},{10,14},{3,7},{... | collective-permute-start | bytes 49160 | tf_op jit(solution)/shard_map/ppermute | solution.py:12
  125.2 5.1 collective-permute-start.2
  130.6 5.1 collective-permute-start.3
  176.8 190.0 %reduce-scatter.9.cloned.1.call-start = ((), (), s32[]{:S(2)}) async-start(), calls=%async_computation.6 | async-start | bytes 294912 | tf_op jit(solution)/shard_map/reduce_scatter | solution.py:57
  177.1 11.8 %collective-permute-start.4 = (bf16[1,64,128]{2,1,0:T(8,128)(2,1)S(1)}, bf16[1,64,128]{2,1,0:T(8,128)(2,1)S(1)}, u32[]{:S(2)}, u32[]{:S(2)}) collective-permute-start(bf16[1,64,128]{2,1,0:T(8,128)(2,1)S(1)} %fusion.93), channel_id=1, source_target_pairs={{4,0},{8,4},{12,8},{5,1},{9,5},{13,9},{6,2},{10,6},{14,10},{7,3},{... | collective-permute-start | bytes 49160 | tf_op jit(solution)/shard_map/ppermute | solution.py:12
  243.0 6.4 %collective-permute-start.5 = (bf16[1,64,128]{2,1,0:T(8,128)(2,1)S(1)}, bf16[1,64,128]{2,1,0:T(8,128)(2,1)S(1)}, u32[]{:S(2)}, u32[]{:S(2)}) collective-permute-start(bf16[1,64,128]{2,1,0:T(8,128)(2,1)S(1)} %get-tuple-element.14), channel_id=1, source_target_pairs={{0,4},{4,8},{8,12},{1,5},{5,9},{9,13},{2,6},{6,10},{10,14},{3,7},{... | collective-permute-start | bytes 49160 | tf_op jit(solution)/shard_map/ppermute | solution.py:12
  249.7 5.1 collective-permute-start.6
  255.1 5.1 collective-permute-start.7
  301.6 189.7 %reduce-scatter.11.cloned.1.call-start = ((), (), s32[]{:S(2)}) async-start(), calls=%async_computation.7 | async-start | bytes 294912 | tf_op jit(solution)/shard_map/reduce_scatter | solution.py:57
  301.8 11.8 %collective-permute-start.8 = (bf16[1,64,128]{2,1,0:T(8,128)(2,1)S(1)}, bf16[1,64,128]{2,1,0:T(8,128)(2,1)S(1)}, u32[]{:S(2)}, u32[]{:S(2)}) collective-permute-start(bf16[1,64,128]{2,1,0:T(8,128)(2,1)S(1)} %fusion.94), channel_id=1, source_target_pairs={{4,0},{8,4},{12,8},{5,1},{9,5},{13,9},{6,2},{10,6},{14,10},{7,3},{... | collective-permute-start | bytes 49160 | tf_op jit(solution)/shard_map/ppermute | solution.py:12
  367.7 6.4 %collective-permute-start.9 = (bf16[1,64,128]{2,1,0:T(8,128)(2,1)S(1)}, bf16[1,64,128]{2,1,0:T(8,128)(2,1)S(1)}, u32[]{:S(2)}, u32[]{:S(2)}) collective-permute-start(bf16[1,64,128]{2,1,0:T(8,128)(2,1)S(1)} %get-tuple-element.22), channel_id=1, source_target_pairs={{0,4},{4,8},{8,12},{1,5},{5,9},{9,13},{2,6},{6,10},{10,14},{3,7},{... | collective-permute-start | bytes 49160 | tf_op jit(solution)/shard_map/ppermute | solution.py:12
  374.4 5.1 collective-permute-start.10
  379.7 5.1 collective-permute-start.11
  426.3 11.7 %collective-permute-start.12 = (bf16[1,64,128]{2,1,0:T(8,128)(2,1)S(1)}, bf16[1,64,128]{2,1,0:T(8,128)(2,1)S(1)}, u32[]{:S(2)}, u32[]{:S(2)}) collective-permute-start(bf16[1,64,128]{2,1,0:T(8,128)(2,1)S(1)} %fusion.95), channel_id=1, source_target_pairs={{4,0},{8,4},{12,8},{5,1},{9,5},{13,9},{6,2},{10,6},{14,10},{7,3},{... | collective-permute-start | bytes 49160 | tf_op jit(solution)/shard_map/ppermute | solution.py:12
  492.2 6.4 %collective-permute-start.13 = (bf16[1,64,128]{2,1,0:T(8,128)(2,1)S(1)}, bf16[1,64,128]{2,1,0:T(8,128)(2,1)S(1)}, u32[]{:S(2)}, u32[]{:S(2)}) collective-permute-start(bf16[1,64,128]{2,1,0:T(8,128)(2,1)S(1)} %get-tuple-element.30), channel_id=1, source_target_pairs={{0,4},{4,8},{8,12},{1,5},{5,9},{9,13},{2,6},{6,10},{10,14},{3,7},{... | collective-permute-start | bytes 49160 | tf_op jit(solution)/shard_map/ppermute | solution.py:12
  498.9 5.1 collective-permute-start.14
  504.2 5.1 collective-permute-start.15
  (3 other events, 10.5 us)
Sparse Core Ops, SparseCore 0:
  51.2 66.3 reduce-scatter.4
  176.9 65.1 reduce-scatter.6
  301.7 65.0 reduce-scatter.8
  426.2 65.0 reduce-scatter.10
where the time goes:
time: 518 us; the launch traced here: 517 us
  waiting for transfers between devices  244 us (47%)
  blocking collectives  99.9 us (19%)
  starting transfers between devices  83.2 us (16%)
  matrix products  60.5 us (12%)
  between operations  13.6 us (3%)
  local copies, waits for them, and re-layouts  9.61 us (2%)
  other arithmetic  5.62 us (1%)
    reduce_scatter x4, waiting for transfers between devices, body(): lax.psum_scatter(terms, ('sub', 'iface'), scatter_dimension=0, tiled=True)  215 us
    all_gather x4, blocking collectives, body(): lax.all_gather(temps_now.astype(jnp.bfloat16), ('sub', 'iface'), axis=0,...  99.9 us
    ppermute x16, starting transfers between devices, from_behind(): return lax.ppermute(block, axis, route)  83.1 us
    dot_general x4, matrix products, body(): jnp.dot(inverse, interior_in, preferred_element_type=jnp.float32)  43.1 us
    ppermute x16, waiting for transfers between devices, from_behind(): return lax.ppermute(block, axis, route)  29.3 us
  transfers between devices with their start and end apart: 20, of which 20 were waited for; matrix products, arithmetic and copies ran while one was open for 0% of the time, Pallas kernels for 0%

commit v1 on v0

--- a/solution.py
+++ b/solution.py
@@ -34,9 +34,16 @@
     couple_f = couple[0].astype(jnp.float32)
     temps_now = previous
     for sweep_index in range(SWEEPS):
-        gathered = lax.all_gather(
-            temps_now.astype(jnp.bfloat16), ("sub", "iface"), axis=0, tiled=True
-        )
+        x = temps_now.astype(jnp.bfloat16)
+        ways, here = (lax.axis_size(("sub", "iface")), lax.axis_index(("sub", "iface")))
+        grown, reach = (x, 1)
+        while reach < ways:
+            theirs = lax.ppermute(grown, ("sub", "iface"), [(d, d ^ reach) for d in range(ways)])
+            mine_first = jnp.concatenate([grown, theirs], axis=0)
+            theirs_first = jnp.concatenate([theirs, grown], axis=0)
+            grown = jnp.where(here & reach == 0, mine_first, theirs_first)
+            reach = 2 * reach
+        gathered = grown
         sub_rows = jnp.take(gathered, block_list, axis=0).reshape(bnd_width, load_count)
         interior_in = jnp.dot(coupled, sub_rows, preferred_element_type=jnp.float32).astype(
             jnp.bfloat16

time: 518 us -> 446 us (0.86)
  blocking collectives: 99.9 us -> 0 us
  waiting for transfers between devices: 244 us -> 267 us
  starting transfers between devices: 83.2 us -> 89 us
    all_gather x4 -> x0, blocking collectives: 99.9 us -> none  [body(): lax.all_gather(temps_now.astype(jnp.bfloat16), ('sub', 'iface'), axis=0,...]
    ppermute x0 -> x12, waiting for transfers between devices: none -> 21.6 us  [body(): lax.ppermute(grown, ('sub', 'iface'), [(d, d ^ reach) for d in range(ways)])]
    ppermute x0 -> x12, starting transfers between devices: none -> 16.7 us  [body(): lax.ppermute(grown, ('sub', 'iface'), [(d, d ^ reach) for d in range(ways)])]
    ppermute x16, starting transfers between devices: 83.1 us -> 72.2 us  [from_behind(): return lax.ppermute(block, axis, route)]
  transfers between devices with their start and end apart: 20 -> 32, of which waited for: 20 -> 32; matrix products, arithmetic and copies ran while one was open for 0% -> 0% of each run, Pallas kernels for 0% -> 0%
where the time goes in v1:
time: 446 us; the launch traced here: 445 us
  waiting for transfers between devices  267 us (60%)
  starting transfers between devices  89 us (20%)
  matrix products  60.6 us (14%)
  between operations  13.7 us (3%)
  local copies, waits for them, and re-layouts  9.6 us (2%)
  other arithmetic  5.74 us (1%)
    reduce_scatter x4, waiting for transfers between devices, body(): lax.psum_scatter(terms, ('sub', 'iface'), scatter_dimension=0, tiled=True)  216 us
    ppermute x16, starting transfers between devices, from_behind(): return lax.ppermute(block, axis, route)  72.2 us
    dot_general x4, matrix products, body(): jnp.dot(inverse, interior_in, preferred_element_type=jnp.float32)  43.1 us
    ppermute x16, waiting for transfers between devices, from_behind(): return lax.ppermute(block, axis, route)  29 us
    ppermute x12, waiting for transfers between devices, body(): lax.ppermute(grown, ('sub', 'iface'), [(d, d ^ reach) for d in range(ways)])  21.6 us
    ppermute x12, starting transfers between devices, body(): lax.ppermute(grown, ('sub', 'iface'), [(d, d ^ reach) for d in range(ways)])  16.7 us
  transfers between devices with their start and end apart: 32, of which 32 were waited for; matrix products, arithmetic and copies ran while one was open for 0% of the time, Pallas kernels for 0%

profile of v1, /device:TPU:1, one launch (start us, length us, event | category | flops | bytes accessed | tf_op | source)
XLA Modules:
  0.0 445.2 jit_solution(1951553102836678632)
XLA Ops:
  18.4 10.8 %fusion.8 = bf16[128,2560]{1,0:T(8,128)(2,1)} fusion(bf16[1,1,2560,2560]{3,2,1,0:T(8,128)(2,1)} %param.17, bf16[512,128]{1,0:T(8,128)(2,1)S(1)} %bitcast.529, bf16[1,1,2560,512]{3,2,1,0:T(8,128)(2,1)S(1)} %copy-done), kind=kOutput, calls=%fused_computation.12 | convolution fusion | flops 2013921280 | bytes 16515072 | tf_op jit(solution)/shard_map/dot_general | solution.py:51
  34.5 5.8 %collective-permute-start.3 = (bf16[1,64,128]{2,1,0:T(8,128)(2,1)S(1)}, bf16[1,64,128]{2,1,0:T(8,128)(2,1)S(1)}, u32[]{:S(2)}, u32[]{:S(2)}) collective-permute-start(bf16[1,64,128]{2,1,0:T(8,128)(2,1)S(1)} %fusion.92), channel_id=1, source_target_pairs={{4,0},{8,4},{12,8},{5,1},{9,5},{13,9},{6,2},{10,6},{14,10},{7,3},{... | collective-permute-start | bytes 49160 | tf_op jit(solution)/shard_map/ppermute | solution.py:12
  43.1 55.5 %reduce-scatter.5.cloned.1.call-done = f32[1,64,128]{2,1,0:T(8,128)} async-done(((f32[8,64,128]{2,1,0:T(8,128)}), f32[1,64,128]{2,1,0:T(8,128)}) %reduce-scatter.5.cloned.1.call-update) | async-done | bytes 32784 | tf_op jit(solution)/shard_map/reduce_scatter | solution.py:64
  99.6 5.6 %collective-permute-start.4 = (bf16[1,64,128]{2,1,0:T(8,128)(2,1)S(1)}, bf16[1,64,128]{2,1,0:T(8,128)(2,1)S(1)}, u32[]{:S(2)}, u32[]{:S(2)}) collective-permute-start(bf16[1,64,128]{2,1,0:T(8,128)(2,1)S(1)} %get-tuple-element.6), channel_id=1, source_target_pairs={{0,4},{4,8},{8,12},{1,5},{5,9},{9,13},{2,6},{6,10},{10,14},{3,7},{... | collective-permute-start | bytes 49160 | tf_op jit(solution)/shard_map/ppermute | solution.py:12
  106.3 4.2 collective-permute-start.5
  111.6 4.2 collective-permute-start.6
  127.5 10.8 %fusion.11 = bf16[128,2560]{1,0:T(8,128)(2,1)} fusion(bf16[1,1,2560,2560]{3,2,1,0:T(8,128)(2,1)} %param.17, bf16[512,128]{1,0:T(8,128)(2,1)S(1)} %bitcast.531, bf16[1,1,2560,512]{3,2,1,0:T(8,128)(2,1)S(1)} %copy-done), kind=kOutput, calls=%fused_computation.13 | convolution fusion | flops 2013921280 | bytes 16515072 | tf_op jit(solution)/shard_map/dot_general | solution.py:51
  146.9 5.4 %collective-permute-done.10 = bf16[1,64,128]{2,1,0:T(8,128)(2,1)S(1)} collective-permute-done((bf16[1,64,128]{2,1,0:T(8,128)(2,1)S(1)}, bf16[1,64,128]{2,1,0:T(8,128)(2,1)S(1)}, u32[]{:S(2)}, u32[]{:S(2)}) %collective-permute-start.10) | collective-permute-done | bytes 16416 | tf_op jit(solution)/shard_map/ppermute | solution.py:12
  152.2 53.5 %reduce-scatter.7.cloned.1.call-done = f32[1,64,128]{2,1,0:T(8,128)} async-done(((f32[8,64,128]{2,1,0:T(8,128)}), f32[1,64,128]{2,1,0:T(8,128)}) %reduce-scatter.7.cloned.1.call-update) | async-done | bytes 32784 | tf_op jit(solution)/shard_map/reduce_scatter | solution.py:64
  206.6 5.6 %collective-permute-start.11 = (bf16[1,64,128]{2,1,0:T(8,128)(2,1)S(1)}, bf16[1,64,128]{2,1,0:T(8,128)(2,1)S(1)}, u32[]{:S(2)}, u32[]{:S(2)}) collective-permute-start(bf16[1,64,128]{2,1,0:T(8,128)(2,1)S(1)} %get-tuple-element.14), channel_id=1, source_target_pairs={{0,4},{4,8},{8,12},{1,5},{5,9},{9,13},{2,6},{6,10},{10,14},{3,7},{... | collective-permute-start | bytes 49160 | tf_op jit(solution)/shard_map/ppermute | solution.py:12
  213.3 4.2 collective-permute-start.12
  218.7 4.4 collective-permute-start.13
  234.5 10.8 %fusion.14 = bf16[128,2560]{1,0:T(8,128)(2,1)} fusion(bf16[1,1,2560,2560]{3,2,1,0:T(8,128)(2,1)} %param.17, bf16[512,128]{1,0:T(8,128)(2,1)S(1)} %bitcast.533, bf16[1,1,2560,512]{3,2,1,0:T(8,128)(2,1)S(1)} %copy-done), kind=kOutput, calls=%fused_computation.14 | convolution fusion | flops 2013921280 | bytes 16515072 | tf_op jit(solution)/shard_map/dot_general | solution.py:51
  253.9 5.4 %collective-permute-done.17 = bf16[1,64,128]{2,1,0:T(8,128)(2,1)S(1)} collective-permute-done((bf16[1,64,128]{2,1,0:T(8,128)(2,1)S(1)}, bf16[1,64,128]{2,1,0:T(8,128)(2,1)S(1)}, u32[]{:S(2)}, u32[]{:S(2)}) %collective-permute-start.17) | collective-permute-done | bytes 16416 | tf_op jit(solution)/shard_map/ppermute | solution.py:12
  259.3 53.5 %reduce-scatter.9.cloned.1.call-done = f32[1,64,128]{2,1,0:T(8,128)} async-done(((f32[8,64,128]{2,1,0:T(8,128)}), f32[1,64,128]{2,1,0:T(8,128)}) %reduce-scatter.9.cloned.1.call-update) | async-done | bytes 32784 | tf_op jit(solution)/shard_map/reduce_scatter | solution.py:64
  313.7 5.5 %collective-permute-start.18 = (bf16[1,64,128]{2,1,0:T(8,128)(2,1)S(1)}, bf16[1,64,128]{2,1,0:T(8,128)(2,1)S(1)}, u32[]{:S(2)}, u32[]{:S(2)}) collective-permute-start(bf16[1,64,128]{2,1,0:T(8,128)(2,1)S(1)} %get-tuple-element.22), channel_id=1, source_target_pairs={{0,4},{4,8},{8,12},{1,5},{5,9},{9,13},{2,6},{6,10},{10,14},{3,7},{... | collective-permute-start | bytes 49160 | tf_op jit(solution)/shard_map/ppermute | solution.py:12
  320.4 4.2 collective-permute-start.19
  325.7 4.2 collective-permute-start.20
  341.6 10.8 %fusion.17 = bf16[128,2560]{1,0:T(8,128)(2,1)} fusion(bf16[1,1,2560,2560]{3,2,1,0:T(8,128)(2,1)} %param.17, bf16[512,128]{1,0:T(8,128)(2,1)S(1)} %bitcast.527, bf16[1,1,2560,512]{3,2,1,0:T(8,128)(2,1)S(1)} %copy-done), kind=kOutput, calls=%fused_computation.15 | convolution fusion | flops 2013921280 | bytes 16515072 | tf_op jit(solution)/shard_map/dot_general | solution.py:51
  360.9 5.4 %collective-permute-done.24 = bf16[1,64,128]{2,1,0:T(8,128)(2,1)S(1)} collective-permute-done((bf16[1,64,128]{2,1,0:T(8,128)(2,1)S(1)}, bf16[1,64,128]{2,1,0:T(8,128)(2,1)S(1)}, u32[]{:S(2)}, u32[]{:S(2)}) %collective-permute-start.24) | collective-permute-done | bytes 16416 | tf_op jit(solution)/shard_map/ppermute | solution.py:12
  366.3 53.5 %reduce-scatter.11.cloned.1.call-done = f32[1,64,128]{2,1,0:T(8,128)} async-done(((f32[8,64,128]{2,1,0:T(8,128)}), f32[1,64,128]{2,1,0:T(8,128)}) %reduce-scatter.11.cloned.1.call-update) | async-done | bytes 32784 | tf_op jit(solution)/shard_map/reduce_scatter | solution.py:64
  420.7 5.6 %collective-permute-start.25 = (bf16[1,64,128]{2,1,0:T(8,128)(2,1)S(1)}, bf16[1,64,128]{2,1,0:T(8,128)(2,1)S(1)}, u32[]{:S(2)}, u32[]{:S(2)}) collective-permute-start(bf16[1,64,128]{2,1,0:T(8,128)(2,1)S(1)} %get-tuple-element.30), channel_id=1, source_target_pairs={{0,4},{4,8},{8,12},{1,5},{5,9},{9,13},{2,6},{6,10},{10,14},{3,7},{... | collective-permute-start | bytes 49160 | tf_op jit(solution)/shard_map/ppermute | solution.py:12
  427.4 4.2 collective-permute-start.26
  432.8 4.2 collective-permute-start.27
  (142 shorter events, 94.4 us)
Async XLA Ops:
  6.5 92.1 %reduce-scatter.5.cloned.1.call-start = ((), (), s32[]{:S(2)}) async-start(), calls=%async_computation.4 | async-start | bytes 294912 | tf_op jit(solution)/shard_map/reduce_scatter | solution.py:64
  10.7 3.8 collective-permute-start.1
  34.2 171.5 %reduce-scatter.7.cloned.1.call-start = ((), (), s32[]{:S(2)}) async-start(), calls=%async_computation.5 | async-start | bytes 294912 | tf_op jit(solution)/shard_map/reduce_scatter | solution.py:64
  34.5 8.6 %collective-permute-start.3 = (bf16[1,64,128]{2,1,0:T(8,128)(2,1)S(1)}, bf16[1,64,128]{2,1,0:T(8,128)(2,1)S(1)}, u32[]{:S(2)}, u32[]{:S(2)}) collective-permute-start(bf16[1,64,128]{2,1,0:T(8,128)(2,1)S(1)} %fusion.92), channel_id=1, source_target_pairs={{4,0},{8,4},{12,8},{5,1},{9,5},{13,9},{6,2},{10,6},{14,10},{7,3},{... | collective-permute-start | bytes 49160 | tf_op jit(solution)/shard_map/ppermute | solution.py:12
  99.6 6.4 %collective-permute-start.4 = (bf16[1,64,128]{2,1,0:T(8,128)(2,1)S(1)}, bf16[1,64,128]{2,1,0:T(8,128)(2,1)S(1)}, u32[]{:S(2)}, u32[]{:S(2)}) collective-permute-start(bf16[1,64,128]{2,1,0:T(8,128)(2,1)S(1)} %get-tuple-element.6), channel_id=1, source_target_pairs={{0,4},{4,8},{8,12},{1,5},{5,9},{9,13},{2,6},{6,10},{10,14},{3,7},{... | collective-permute-start | bytes 49160 | tf_op jit(solution)/shard_map/ppermute | solution.py:12
  106.3 5.1 %collective-permute-start.5 = (bf16[1,64,128]{2,1,0:T(8,128)(2,1)S(1)}, bf16[1,64,128]{2,1,0:T(8,128)(2,1)S(1)}, u32[]{:S(2)}, u32[]{:S(2)}) collective-permute-start(bf16[1,64,128]{2,1,0:T(8,128)(2,1)S(1)} %get-tuple-element.8), channel_id=1, source_target_pairs={{0,4},{4,8},{8,12},{1,5},{5,9},{9,13},{2,6},{6,10},{10,14},{3,7},{... | collective-permute-start | bytes 49160 | tf_op jit(solution)/shard_map/ppermute | solution.py:12
  111.6 5.1 %collective-permute-start.6 = (bf16[1,64,128]{2,1,0:T(8,128)(2,1)S(1)}, bf16[1,64,128]{2,1,0:T(8,128)(2,1)S(1)}, u32[]{:S(2)}, u32[]{:S(2)}) collective-permute-start(bf16[1,64,128]{2,1,0:T(8,128)(2,1)S(1)} %get-tuple-element.10), channel_id=1, source_target_pairs={{0,4},{4,8},{8,12},{1,5},{5,9},{9,13},{2,6},{6,10},{10,14},{3,7},{... | collective-permute-start | bytes 49160 | tf_op jit(solution)/shard_map/ppermute | solution.py:12
  119.6 4.0 collective-permute-start.8
  143.1 169.6 %reduce-scatter.9.cloned.1.call-start = ((), (), s32[]{:S(2)}) async-start(), calls=%async_computation.6 | async-start | bytes 294912 | tf_op jit(solution)/shard_map/reduce_scatter | solution.py:64
  143.4 8.8 %collective-permute-start.10 = (bf16[1,64,128]{2,1,0:T(8,128)(2,1)S(1)}, bf16[1,64,128]{2,1,0:T(8,128)(2,1)S(1)}, u32[]{:S(2)}, u32[]{:S(2)}) collective-permute-start(bf16[1,64,128]{2,1,0:T(8,128)(2,1)S(1)} %fusion.93), channel_id=1, source_target_pairs={{4,0},{8,4},{12,8},{5,1},{9,5},{13,9},{6,2},{10,6},{14,10},{7,3},{... | collective-permute-start | bytes 49160 | tf_op jit(solution)/shard_map/ppermute | solution.py:12
  206.6 6.4 %collective-permute-start.11 = (bf16[1,64,128]{2,1,0:T(8,128)(2,1)S(1)}, bf16[1,64,128]{2,1,0:T(8,128)(2,1)S(1)}, u32[]{:S(2)}, u32[]{:S(2)}) collective-permute-start(bf16[1,64,128]{2,1,0:T(8,128)(2,1)S(1)} %get-tuple-element.14), channel_id=1, source_target_pairs={{0,4},{4,8},{8,12},{1,5},{5,9},{9,13},{2,6},{6,10},{10,14},{3,7},{... | collective-permute-start | bytes 49160 | tf_op jit(solution)/shard_map/ppermute | solution.py:12
  213.3 5.1 %collective-permute-start.12 = (bf16[1,64,128]{2,1,0:T(8,128)(2,1)S(1)}, bf16[1,64,128]{2,1,0:T(8,128)(2,1)S(1)}, u32[]{:S(2)}, u32[]{:S(2)}) collective-permute-start(bf16[1,64,128]{2,1,0:T(8,128)(2,1)S(1)} %get-tuple-element.16), channel_id=1, source_target_pairs={{0,4},{4,8},{8,12},{1,5},{5,9},{9,13},{2,6},{6,10},{10,14},{3,7},{... | collective-permute-start | bytes 49160 | tf_op jit(solution)/shard_map/ppermute | solution.py:12
  218.7 5.1 %collective-permute-start.13 = (bf16[1,64,128]{2,1,0:T(8,128)(2,1)S(1)}, bf16[1,64,128]{2,1,0:T(8,128)(2,1)S(1)}, u32[]{:S(2)}, u32[]{:S(2)}) collective-permute-start(bf16[1,64,128]{2,1,0:T(8,128)(2,1)S(1)} %get-tuple-element.18), channel_id=1, source_target_pairs={{0,4},{4,8},{8,12},{1,5},{5,9},{9,13},{2,6},{6,10},{10,14},{3,7},{... | collective-permute-start | bytes 49160 | tf_op jit(solution)/shard_map/ppermute | solution.py:12
  226.7 4.0 collective-permute-start.15
  250.2 169.6 %reduce-scatter.11.cloned.1.call-start = ((), (), s32[]{:S(2)}) async-start(), calls=%async_computation.7 | async-start | bytes 294912 | tf_op jit(solution)/shard_map/reduce_scatter | solution.py:64
  250.5 8.8 %collective-permute-start.17 = (bf16[1,64,128]{2,1,0:T(8,128)(2,1)S(1)}, bf16[1,64,128]{2,1,0:T(8,128)(2,1)S(1)}, u32[]{:S(2)}, u32[]{:S(2)}) collective-permute-start(bf16[1,64,128]{2,1,0:T(8,128)(2,1)S(1)} %fusion.94), channel_id=1, source_target_pairs={{4,0},{8,4},{12,8},{5,1},{9,5},{13,9},{6,2},{10,6},{14,10},{7,3},{... | collective-permute-start | bytes 49160 | tf_op jit(solution)/shard_map/ppermute | solution.py:12
  313.7 6.4 %collective-permute-start.18 = (bf16[1,64,128]{2,1,0:T(8,128)(2,1)S(1)}, bf16[1,64,128]{2,1,0:T(8,128)(2,1)S(1)}, u32[]{:S(2)}, u32[]{:S(2)}) collective-permute-start(bf16[1,64,128]{2,1,0:T(8,128)(2,1)S(1)} %get-tuple-element.22), channel_id=1, source_target_pairs={{0,4},{4,8},{8,12},{1,5},{5,9},{9,13},{2,6},{6,10},{10,14},{3,7},{... | collective-permute-start | bytes 49160 | tf_op jit(solution)/shard_map/ppermute | solution.py:12
  320.4 5.1 %collective-permute-start.19 = (bf16[1,64,128]{2,1,0:T(8,128)(2,1)S(1)}, bf16[1,64,128]{2,1,0:T(8,128)(2,1)S(1)}, u32[]{:S(2)}, u32[]{:S(2)}) collective-permute-start(bf16[1,64,128]{2,1,0:T(8,128)(2,1)S(1)} %get-tuple-element.24), channel_id=1, source_target_pairs={{0,4},{4,8},{8,12},{1,5},{5,9},{9,13},{2,6},{6,10},{10,14},{3,7},{... | collective-permute-start | bytes 49160 | tf_op jit(solution)/shard_map/ppermute | solution.py:12
  325.7 5.1 %collective-permute-start.20 = (bf16[1,64,128]{2,1,0:T(8,128)(2,1)S(1)}, bf16[1,64,128]{2,1,0:T(8,128)(2,1)S(1)}, u32[]{:S(2)}, u32[]{:S(2)}) collective-permute-start(bf16[1,64,128]{2,1,0:T(8,128)(2,1)S(1)} %get-tuple-element.26), channel_id=1, source_target_pairs={{0,4},{4,8},{8,12},{1,5},{5,9},{9,13},{2,6},{6,10},{10,14},{3,7},{... | collective-permute-start | bytes 49160 | tf_op jit(solution)/shard_map/ppermute | solution.py:12
  333.7 4.0 collective-permute-start.22
  357.4 8.8 %collective-permute-start.24 = (bf16[1,64,128]{2,1,0:T(8,128)(2,1)S(1)}, bf16[1,64,128]{2,1,0:T(8,128)(2,1)S(1)}, u32[]{:S(2)}, u32[]{:S(2)}) collective-permute-start(bf16[1,64,128]{2,1,0:T(8,128)(2,1)S(1)} %fusion.95), channel_id=1, source_target_pairs={{4,0},{8,4},{12,8},{5,1},{9,5},{13,9},{6,2},{10,6},{14,10},{7,3},{... | collective-permute-start | bytes 49160 | tf_op jit(solution)/shard_map/ppermute | solution.py:12
  420.7 6.4 %collective-permute-start.25 = (bf16[1,64,128]{2,1,0:T(8,128)(2,1)S(1)}, bf16[1,64,128]{2,1,0:T(8,128)(2,1)S(1)}, u32[]{:S(2)}, u32[]{:S(2)}) collective-permute-start(bf16[1,64,128]{2,1,0:T(8,128)(2,1)S(1)} %get-tuple-element.30), channel_id=1, source_target_pairs={{0,4},{4,8},{8,12},{1,5},{5,9},{9,13},{2,6},{6,10},{10,14},{3,7},{... | collective-permute-start | bytes 49160 | tf_op jit(solution)/shard_map/ppermute | solution.py:12
  427.4 5.1 %collective-permute-start.26 = (bf16[1,64,128]{2,1,0:T(8,128)(2,1)S(1)}, bf16[1,64,128]{2,1,0:T(8,128)(2,1)S(1)}, u32[]{:S(2)}, u32[]{:S(2)}) collective-permute-start(bf16[1,64,128]{2,1,0:T(8,128)(2,1)S(1)} %get-tuple-element.32), channel_id=1, source_target_pairs={{0,4},{4,8},{8,12},{1,5},{5,9},{9,13},{2,6},{6,10},{10,14},{3,7},{... | collective-permute-start | bytes 49160 | tf_op jit(solution)/shard_map/ppermute | solution.py:12
  432.8 5.1 %collective-permute-start.27 = (bf16[1,64,128]{2,1,0:T(8,128)(2,1)S(1)}, bf16[1,64,128]{2,1,0:T(8,128)(2,1)S(1)}, u32[]{:S(2)}, u32[]{:S(2)}) collective-permute-start(bf16[1,64,128]{2,1,0:T(8,128)(2,1)S(1)} %get-tuple-element.34), channel_id=1, source_target_pairs={{0,4},{4,8},{8,12},{1,5},{5,9},{9,13},{2,6},{6,10},{10,14},{3,7},{... | collective-permute-start | bytes 49160 | tf_op jit(solution)/shard_map/ppermute | solution.py:12
  (15 other events, 190.9 us)
Sparse Core Ops, SparseCore 0:
  34.3 64.2 reduce-scatter.4
  143.3 62.4 reduce-scatter.6
  250.3 62.4 reduce-scatter.8
  357.3 62.4 reduce-scatter.10
